TPU v7x, 512 devices: a whole 4x8x8 slice. The times are simulated.
512 devices in a mesh: tm: 16 (over y, core), pre: 32 (over z, x).
Axes of the slice: x: 4, y: 8, z: 8, core: 2. Of those that a mesh axis runs over, the one named last changes fastest.
Arguments:
- spikes: int32 [3072, 16384], P('tm', 'pre'), may hold values from 0 to 1
- trace_decay: float32 [16384], P('pre'), may hold values from 0.96 to 1
- pseudo_deriv: bfloat16 [3072, 16384], P('pre', 'tm'), may hold values from 0 to 0.29882812
- readout_weight: bfloat16 [16384, 512], P('pre'), may hold values from -2 to 2
- feedback_weight: bfloat16 [16384, 512], P('tm'), may hold values from -6 to 6
- targets: int32 [3072], P('tm'), may hold values from 0 to 511
Outputs:
- gradient: float32 [16384, 16384], P('pre', 'tm')
All inputs are finite; a program needn't handle non-finite values.
Results may differ from a plain program's by a relative error of at most 0.0022.
Values may be sent and summed in bfloat16 or wider, within the bound.
No kernel may reach another device: no remote copies, remote signals or barrier semaphores. Data moves between devices by JAX's collectives and lax.ppermute only.
A program may use at most 64 MiB of HBM per device.

v0:
```python
import jax
import jax.numpy as jnp
from jax import lax
from jax.sharding import Mesh, PartitionSpec as P

NZ = 8
PRE = ("z", "x")


def combine_pairs(earlier, later):
    return (earlier[0] * later[0], later[1] + later[0] * earlier[1])


def local_traces(spikes, decays):
    factor = jnp.broadcast_to(decays[None, :], spikes.shape)
    source = (1.0 - decays)[None, :] * spikes.astype(jnp.float32)
    return lax.associative_scan(combine_pairs, (factor, source), axis=0)


def pre_size():
    return lax.axis_size("z") * lax.axis_size("x")


def pre_index():
    return lax.axis_index("z") * lax.axis_size("x") + lax.axis_index("x")


def owned_errors(spikes, readout_weight, targets):
    npre = pre_size()
    b = pre_index()
    partial_logits = jnp.dot(
        spikes.astype(jnp.bfloat16), readout_weight, preferred_element_type=jnp.float32
    )
    rows = partial_logits.shape[0] // npre
    pieces = lax.all_to_all(partial_logits, PRE, 0, 0, tiled=True)
    logits = pieces.reshape(npre, rows, -1).sum(0)
    class_prob = jax.nn.softmax(logits, axis=-1)
    classes = lax.broadcasted_iota(jnp.int32, logits.shape, 1)
    mine = lax.dynamic_slice_in_dim(targets, b * rows, rows, 0)
    onehot = (mine[:, None] == classes).astype(jnp.float32)
    return (class_prob - onehot).astype(jnp.bfloat16)


def route_errors(errors, ntm, npre, deriv_rows):
    rows = errors.shape[0]
    tstep = rows * npre
    per = deriv_rows // rows
    perm = []
    for a in range(ntm):
        for b in range(npre):
            start = tstep * a + rows * b
            dst_b = start // deriv_rows
            dst_a = start % deriv_rows // rows
            perm.append((a * npre + b, dst_a * npre + dst_b))
    moved = lax.ppermute(errors, ("tm",) + PRE, perm)
    assert per == ntm
    return lax.all_gather(moved, "tm", axis=0, tiled=True)


def ring_gather(block, axis, count):
    index = lax.axis_index(axis)
    fwd = [(i, (i + 1) % count) for i in range(count)]
    bwd = [(i, (i - 1) % count) for i in range(count)]
    out = jnp.zeros((count,) + block.shape, block.dtype)
    out = lax.dynamic_update_slice_in_dim(out, block[None], index, 0)
    f = block
    b = block
    for s in range(1, count // 2 + 1):
        f = lax.ppermute(f, axis, fwd)
        out = lax.dynamic_update_slice_in_dim(out, f[None], (index - s) % count, 0)
        if s < count - count // 2:
            b = lax.ppermute(b, axis, bwd)
            out = lax.dynamic_update_slice_in_dim(out, b[None], (index + s) % count, 0)
    return out.reshape((count * block.shape[0],) + block.shape[1:])


def ring_stage(block, axis, count, fwd, bwd):
    coord = lax.axis_index(axis)
    pieces = [None] * count
    pieces[0] = block
    f = block
    r = block
    for s in range(1, count // 2 + 1):
        f = lax.ppermute(f, axis, fwd)
        pieces[count - s] = f
        if s < count - count // 2:
            r = lax.ppermute(r, axis, bwd)
            pieces[s] = r
    stacked = jnp.stack(pieces + pieces, 0)
    return lax.dynamic_slice_in_dim(stacked, (count - coord) % count, count, 0)


def weighted_gather(weighted):
    nz = lax.axis_size("z")
    nx = lax.axis_size("x")
    half = weighted.shape[1] // 2
    rows = nz * nx * weighted.shape[0]
    first = lax.all_gather(weighted[:, :half], "x", axis=0, tiled=True)
    first = lax.all_gather(first, "z", axis=0, tiled=True)
    zf = [(i, (i + 1) % nz) for i in range(nz)]
    zb = [(i, (i - 1) % nz) for i in range(nz)]
    xf = [(i, (i + 1) % nx) for i in range(nx)]
    xb = [(i, (i - 1) % nx) for i in range(nx)]
    second = ring_stage(ring_stage(weighted[:, half:], "z", nz, zf, zb), "x", nx, xf, xb)
    second = jnp.swapaxes(second, 0, 1)
    return (first, second.reshape(rows, -1))


def shards(spikes, trace_decay, pseudo_deriv, readout_weight, feedback_weight, targets):
    ntm = lax.axis_size("tm")
    npre = pre_size()
    a = lax.axis_index("tm")
    errors = owned_errors(spikes, readout_weight, targets)
    err_rows = route_errors(errors, ntm, npre, pseudo_deriv.shape[0])
    signal = lax.dot_general(
        err_rows, feedback_weight, (((1,), (1,)), ((), ())), preferred_element_type=jnp.float32
    )
    weighted = (signal * pseudo_deriv.astype(jnp.float32)).astype(jnp.bfloat16)
    left_all, right_all = weighted_gather(weighted)
    powers, states = local_traces(spikes, trace_decay)
    ends = lax.all_gather(states[-1], "tm", axis=0)
    span = powers[-1]

    def step(k, carry):
        return jnp.where(k < a, span * carry + ends[k], carry)

    incoming = lax.fori_loop(0, ntm, step, jnp.zeros_like(trace_decay))
    traces = (states + powers * incoming[None, :]).astype(jnp.bfloat16)
    traces_all = ring_gather(traces, "tm", ntm)
    left = outer_sum(traces_all, left_all)
    right = outer_sum(traces_all, right_all)
    return jnp.concatenate([left, right], 1)


def outer_sum(left_rows, right_rows):
    return lax.dot_general(
        left_rows, right_rows, (((0,), (0,)), ((), ())), preferred_element_type=jnp.float32
    )


def solution(mesh):
    ntm, npre = mesh.devices.shape
    assert npre % NZ == 0
    plane = Mesh(mesh.devices.reshape(ntm, NZ, npre // NZ), ("tm",) + PRE)
    placed = (P("tm", PRE), P(PRE), P(PRE, "tm"), P(PRE, None), P("tm", None), P("tm"))
    return jax.shard_map(
        shards, mesh=plane, in_specs=placed, out_specs=P(PRE, "tm"), check_vma=False
    )
```

profile of v0, /device:TPU:16, one launch (start us, length us, event | category | flops | bytes accessed | tf_op | source)
XLA Modules:
  0.0 224.9 jit_solution(6964825766229947155)
XLA Ops:
  6.5 0.8 broadcast_subtract_fusion
  7.3 1.0 convert_multiply_fusion
  8.6 0.7 multiply_add_fusion
  11.6 17.3 %all-gather = f32[16,1,512]{2,1,0:T(1,128)S(1)} all-gather(f32[1,1,512]{2,1,0:T(1,128)S(1)} %add_bitcast_fusion), channel_id=1, replica_groups=mesh['tm'=16,'z'=8,'x'=4] {'tm'}, dimensions={0}, use_global_device_ids=true | all-gather | bytes 34816 | tf_op jit(solution)/shard_map/all_gather | solution.py:121
  29.7 12.1 %while.14 = (s32[]{:T(128)}, f32[512]{0:T(512)S(1)}, s32[]{:T(128)}, f32[512]{0:T(512)S(1)}, f32[16,512]{1,0:T(8,128)}, /*index=5*/s32[]{:T(128)}, s32[]{:T(128)}) while((s32[]{:T(128)}, f32[512]{0:T(512)S(1)}, s32[]{:T(128)}, f32[512]{0:T(512)S(1)}, f32[16,512]{1,0:T(8,128)}, /*index=5*/s32[]{:T(128)}, s32[]{:T(128)}) %tuple.58), condition=%wide.region_1.0_spmd.clone, body=%wide.region_0.0_spmd.clone.sunk | while | flops 2052 | bytes 12389 | solution.py:127
  29.7 0.8 constant_dynamic-slice_fusion.4
  30.5 0.7 constant_dynamic-slice_fusion.4
  31.3 0.7 constant_dynamic-slice_fusion.4
  32.0 0.7 constant_dynamic-slice_fusion.4
  32.8 0.7 constant_dynamic-slice_fusion.4
  33.5 0.7 constant_dynamic-slice_fusion.4
  34.3 0.7 constant_dynamic-slice_fusion.4
  35.0 0.7 constant_dynamic-slice_fusion.4
  35.8 0.7 constant_dynamic-slice_fusion.4
  36.5 0.7 constant_dynamic-slice_fusion.4
  37.3 0.7 constant_dynamic-slice_fusion.4
  38.0 0.7 constant_dynamic-slice_fusion.4
  38.8 0.7 constant_dynamic-slice_fusion.4
  39.5 0.7 constant_dynamic-slice_fusion.4
  40.3 0.7 constant_dynamic-slice_fusion.4
  41.0 0.7 constant_dynamic-slice_fusion.4
  41.8 2.0 broadcast_in_dim.65
  43.8 0.9 bitcast_dynamic-update-slice_fusion.23
  45.0 2.8 %collective-permute-start.1 = (bf16[192,512]{1,0:T(8,128)(2,1)}, bf16[192,512]{1,0:T(8,128)(2,1)S(1)}, u32[]{:S(2)}, u32[]{:S(2)}) collective-permute-start(bf16[192,512]{1,0:T(8,128)(2,1)} %get-tuple-element.131), channel_id=1, source_target_pairs={{0,480},{32,0},{64,32},{96,64},{128,96},{160,128},{192,160},{224,1... | collective-permute-start | bytes 589832 | tf_op jit(solution)/shard_map/ppermute | solution.py:72
  48.1 0.8 all_to_all.6
  49.0 9.8 %all-to-all-start = ((f32[32,6,512]{2,1,0:T(8,128)}), f32[32,6,512]{2,1,0:T(8,128)S(1)}, u32[]{:S(2)}, u32[]{:S(2)}) async-start(f32[32,6,512]{2,1,0:T(8,128)} %all_to_all.6), calls=%async_computation | async-start | bytes 1048576 | tf_op jit(solution)/shard_map/all_to_all | solution.py:35
  59.4 1.7 collective-permute-start.3
  61.7 0.7 bitcast_dynamic-update-slice_fusion.21
  62.4 2.0 collective-permute-done.2
  64.4 1.7 collective-permute-start.5
  67.5 2.0 collective-permute-done.4
  69.5 2.0 collective-permute-start.7
  72.2 4.8 %all-to-all-done = f32[32,6,512]{2,1,0:T(8,128)S(1)} async-done(((f32[32,6,512]{2,1,0:T(8,128)}), f32[32,6,512]{2,1,0:T(8,128)S(1)}, u32[]{:S(2)}, u32[]{:S(2)}) %all-to-all-start) | async-done | bytes 393248 | tf_op jit(solution)/shard_map/all_to_all | solution.py:35
  77.5 7.0 %collective-permute-start.15 = (bf16[6,512]{1,0:T(8,128)(2,1)S(1)}, bf16[6,512]{1,0:T(8,128)(2,1)S(1)}, u32[]{:S(2)}, u32[]{:S(2)}) collective-permute-start(bf16[6,512]{1,0:T(8,128)(2,1)S(1)} %subtract_convert_fusion), channel_id=1, source_target_pairs={{0,0},{1,32},{2,64},{3,96},{4,128},{5,160},{6,192},{7,224},{8,256}... | collective-permute-start | bytes 18440 | tf_op jit(solution)/shard_map/ppermute | solution.py:55
  85.8 18.8 %all-gather.1 = bf16[16,6,512]{2,1,0:T(8,128)(2,1)S(1)} all-gather(bf16[1,6,512]{2,1,0:T(8,128)(2,1)S(1)} %bitcast.112), channel_id=1, replica_groups=mesh['tm'=16,'z'=8,'x'=4] {'tm'}, dimensions={0}, use_global_device_ids=true | all-gather | bytes 104448 | tf_op jit(solution)/shard_map/all_gather | solution.py:57
  105.2 4.9 %collective-permute-start.16 = (bf16[96,512]{1,0:T(8,128)(2,1)S(1)}, bf16[96,512]{1,0:T(8,128)(2,1)S(1)}, u32[]{:S(2)}, u32[]{:S(2)}) collective-permute-start(bf16[96,512]{1,0:T(8,128)(2,1)S(1)} %get-tuple-element.135), channel_id=1, source_target_pairs={{0,28},{4,0},{8,4},{12,8},{16,12},{20,16},{24,20},{28,24},{1,29},{... | collective-permute-start | bytes 294920 | tf_op jit(solution)/shard_map/ppermute | solution.py:87
  110.1 1.9 collective-permute-start.19
  112.0 14.1 %all_gather.14 = bf16[384,512]{1,0:T(8,128)(2,1)} all-gather(bf16[96,512]{1,0:T(8,128)(2,1)S(1)} %get-tuple-element.134), channel_id=1, replica_groups=mesh['tm'=16,'z'=8,'x'=4] {'x'}, dimensions={0}, use_global_device_ids=true | all-gather | bytes 491520 | tf_op jit(solution)/shard_map/all_gather | solution.py:98
  126.3 1.7 collective-permute-start.9
  128.0 0.7 bitcast_dynamic-update-slice_fusion.16
  128.7 0.7 bitcast_dynamic-update-slice_fusion.15
  129.4 5.6 %collective-permute-start.17 = (bf16[96,512]{1,0:T(8,128)(2,1)S(1)}, bf16[96,512]{1,0:T(8,128)(2,1)S(1)}, u32[]{:S(2)}, u32[]{:S(2)}) collective-permute-start(bf16[96,512]{1,0:T(8,128)(2,1)S(1)} %collective-permute-done.16), channel_id=1, source_target_pairs={{0,28},{4,0},{8,4},{12,8},{16,12},{20,16},{24,20},{28,24},{1,29},{... | collective-permute-start | bytes 294920 | tf_op jit(solution)/shard_map/ppermute | solution.py:87
  135.0 1.9 collective-permute-start.20
  137.0 1.2 collective-permute-done.17
  138.1 5.6 %collective-permute-start.18 = (bf16[96,512]{1,0:T(8,128)(2,1)S(1)}, bf16[96,512]{1,0:T(8,128)(2,1)S(1)}, u32[]{:S(2)}, u32[]{:S(2)}) collective-permute-start(bf16[96,512]{1,0:T(8,128)(2,1)S(1)} %collective-permute-done.17), channel_id=1, source_target_pairs={{0,28},{4,0},{8,4},{12,8},{16,12},{20,16},{24,20},{28,24},{1,29},{... | collective-permute-start | bytes 294920 | tf_op jit(solution)/shard_map/ppermute | solution.py:87
  143.7 1.9 collective-permute-start.21
  145.7 1.7 collective-permute-start.11
  147.4 6.7 %collective-permute-done.21 = bf16[96,512]{1,0:T(8,128)(2,1)S(1)} collective-permute-done((bf16[96,512]{1,0:T(8,128)(2,1)S(1)}, bf16[96,512]{1,0:T(8,128)(2,1)S(1)}, u32[]{:S(2)}, u32[]{:S(2)}) %collective-permute-start.21) | collective-permute-done | bytes 98336 | tf_op jit(solution)/shard_map/ppermute | solution.py:84
  154.2 1.9 collective-permute-start.22
  156.1 8.2 %collective-permute-done.22 = bf16[96,512]{1,0:T(8,128)(2,1)S(1)} collective-permute-done((bf16[96,512]{1,0:T(8,128)(2,1)S(1)}, bf16[96,512]{1,0:T(8,128)(2,1)S(1)}, u32[]{:S(2)}, u32[]{:S(2)}) %collective-permute-start.22) | collective-permute-done | bytes 98336 | tf_op jit(solution)/shard_map/ppermute | solution.py:84
  164.7 1.9 collective-permute-start.24
  166.6 0.7 bitcast_dynamic-update-slice_fusion.14
  168.0 5.1 %collective-permute-start.23 = (bf16[8,96,512]{2,1,0:T(8,128)(2,1)S(1)}, bf16[8,96,512]{2,1,0:T(8,128)(2,1)S(1)}, u32[]{:S(2)}, u32[]{:S(2)}) collective-permute-start(bf16[8,96,512]{2,1,0:T(8,128)(2,1)S(1)} %get-tuple-element.129), channel_id=1, source_target_pairs={{0,3},{1,0},{2,1},{3,2},{4,7},{5,4},{6,5},{7,6},{8,11},{9,8},{10,9... | collective-permute-start | bytes 2359304 | tf_op jit(solution)/shard_map/ppermute | solution.py:87
  173.2 1.7 collective-permute-start.13
  175.6 0.7 bitcast_dynamic-update-slice_fusion.11
  176.3 2.0 collective-permute-done.12
  178.3 7.3 %collective-permute-done.24 = bf16[8,96,512]{2,1,0:T(8,128)(2,1)S(1)} collective-permute-done((bf16[8,96,512]{2,1,0:T(8,128)(2,1)S(1)}, bf16[8,96,512]{2,1,0:T(8,128)(2,1)S(1)}, u32[]{:S(2)}, u32[]{:S(2)}) %collective-permute-start.24) | collective-permute-done | bytes 786464 | tf_op jit(solution)/shard_map/ppermute | solution.py:84
  185.6 1.9 collective-permute-start.25
  188.2 0.7 bitcast_dynamic-update-slice_fusion.9
  188.9 0.7 bitcast_dynamic-update-slice_fusion.8
  189.6 15.8 %collective-permute-done.25 = bf16[8,96,512]{2,1,0:T(8,128)(2,1)S(1)} collective-permute-done((bf16[8,96,512]{2,1,0:T(8,128)(2,1)S(1)}, bf16[8,96,512]{2,1,0:T(8,128)(2,1)S(1)}, u32[]{:S(2)}, u32[]{:S(2)}) %collective-permute-start.25) | collective-permute-done | bytes 786464 | tf_op jit(solution)/shard_map/ppermute | solution.py:84
  206.6 4.7 %fusion.19 = f32[512,512]{0,1:T(8,128)} fusion(bf16[3072,512]{1,0:T(8,128)(2,1)} %bitcast.27, bf16[3072,512]{1,0:T(8,128)(2,1)S(1)} %bitcast.98), kind=kOutput, calls=%fused_computation.114 | convolution fusion | flops 1610612736 | bytes 7340032 | tf_op jit(solution)/shard_map/dot_general | solution.py:136
  211.3 4.8 %fusion.18 = f32[512,512]{0,1:T(8,128)S(1)} fusion(bf16[3072,512]{1,0:T(8,128)(2,1)} %bitcast.27, bf16[3072,512]{1,0:T(8,128)(2,1)} %all-gather.4.cloned.1.call-done), kind=kOutput, calls=%fused_computation.113 | convolution fusion | flops 1610612736 | bytes 7340032 | tf_op jit(solution)/shard_map/dot_general | solution.py:136
  216.2 1.8 copy.11
  (197 shorter events, 12.6 us)
Async XLA Ops:
  6.5 98.2 %copy-start = (bf16[1024,512]{1,0:T(8,128)(2,1)S(1)}, bf16[1024,512]{1,0:T(8,128)(2,1)}, u32[]{:S(2)}) copy-start(bf16[1024,512]{1,0:T(8,128)(2,1)} %param.12) | copy-start | bytes 3145732
  8.4 2.4 %copy-start.1 = (f32[192,512]{1,0:T(8,128)}, f32[192,512]{1,0:T(8,128)S(1)}, u32[]{:S(2)}) copy-start(f32[192,512]{1,0:T(8,128)S(1)} %convert_multiply_fusion) | copy-start | bytes 1179652
  10.6 0.7 copy-start.6
  10.8 0.7 slice-start
  29.5 18.3 %copy-start.2 = (s32[192,512]{1,0:T(8,128)S(1)}, s32[192,512]{1,0:T(8,128)}, u32[]{:S(2)}) copy-start(s32[192,512]{1,0:T(8,128)} %param.8) | copy-start | bytes 1179652
  29.7 18.2 %copy-start.4 = (bf16[512,512]{1,0:T(8,128)(2,1)S(1)}, bf16[512,512]{1,0:T(8,128)(2,1)}, u32[]{:S(2)}) copy-start(bf16[512,512]{1,0:T(8,128)(2,1)} %param.11) | copy-start | bytes 1572868
  43.8 15.4 %copy-start.7 = (s32[192]{0:T(256)S(1)}, s32[192]{0:T(256)}, u32[]{:S(2)}) copy-start(s32[192]{0:T(256)} %param.13) | copy-start | bytes 2308
  44.7 14.6 %collective-permute-start = (bf16[192,512]{1,0:T(8,128)(2,1)}, bf16[192,512]{1,0:T(8,128)(2,1)S(1)}, u32[]{:S(2)}, u32[]{:S(2)}) collective-permute-start(bf16[192,512]{1,0:T(8,128)(2,1)} %get-tuple-element.131), channel_id=1, source_target_pairs={{0,32},{32,64},{64,96},{96,128},{128,160},{160,192},{192,224},{224... | collective-permute-start | bytes 589832 | tf_op jit(solution)/shard_map/ppermute | solution.py:69
  45.0 14.3 %collective-permute-start.1 = (bf16[192,512]{1,0:T(8,128)(2,1)}, bf16[192,512]{1,0:T(8,128)(2,1)S(1)}, u32[]{:S(2)}, u32[]{:S(2)}) collective-permute-start(bf16[192,512]{1,0:T(8,128)(2,1)} %get-tuple-element.131), channel_id=1, source_target_pairs={{0,480},{32,0},{64,32},{96,64},{128,96},{160,128},{192,160},{224,1... | collective-permute-start | bytes 589832 | tf_op jit(solution)/shard_map/ppermute | solution.py:72
  48.1 56.6 %copy-start.5 = (bf16[96,1024]{1,0:T(8,128)(2,1)S(1)}, bf16[96,1024]{1,0:T(8,128)(2,1)}, u32[]{:S(2)}) copy-start(bf16[96,1024]{1,0:T(8,128)(2,1)} %param.10) | copy-start | bytes 589828
  49.0 28.1 %all-to-all-start = ((f32[32,6,512]{2,1,0:T(8,128)}), f32[32,6,512]{2,1,0:T(8,128)S(1)}, u32[]{:S(2)}, u32[]{:S(2)}) async-start(f32[32,6,512]{2,1,0:T(8,128)} %all_to_all.6), calls=%async_computation | async-start | bytes 1048576 | tf_op jit(solution)/shard_map/all_to_all | solution.py:35
  58.8 152.5 %all-gather.4.cloned.1.call-start = ((), (), s32[]{:S(2)}) async-start(), calls=%async_computation.1 | async-start | bytes 3538944 | tf_op jit(solution)/shard_map/all_gather | solution.py:99
  59.3 5.1 %collective-permute-start.2 = (bf16[192,512]{1,0:T(8,128)(2,1)S(1)}, bf16[192,512]{1,0:T(8,128)(2,1)S(1)}, u32[]{:S(2)}, u32[]{:S(2)}) collective-permute-start(bf16[192,512]{1,0:T(8,128)(2,1)S(1)} %collective-permute-done), channel_id=1, source_target_pairs={{0,32},{32,64},{64,96},{96,128},{128,160},{160,192},{192,224},{224... | collective-permute-start | bytes 589832 | tf_op jit(solution)/shard_map/ppermute | solution.py:69
  59.4 5.0 %collective-permute-start.3 = (bf16[192,512]{1,0:T(8,128)(2,1)S(1)}, bf16[192,512]{1,0:T(8,128)(2,1)S(1)}, u32[]{:S(2)}, u32[]{:S(2)}) collective-permute-start(bf16[192,512]{1,0:T(8,128)(2,1)S(1)} %collective-permute-done.1), channel_id=1, source_target_pairs={{0,480},{32,0},{64,32},{96,64},{128,96},{160,128},{192,160},{224,1... | collective-permute-start | bytes 589832 | tf_op jit(solution)/shard_map/ppermute | solution.py:72
  64.4 5.1 %collective-permute-start.4 = (bf16[192,512]{1,0:T(8,128)(2,1)S(1)}, bf16[192,512]{1,0:T(8,128)(2,1)S(1)}, u32[]{:S(2)}, u32[]{:S(2)}) collective-permute-start(bf16[192,512]{1,0:T(8,128)(2,1)S(1)} %collective-permute-done.2), channel_id=1, source_target_pairs={{0,32},{32,64},{64,96},{96,128},{128,160},{160,192},{192,224},{224... | collective-permute-start | bytes 589832 | tf_op jit(solution)/shard_map/ppermute | solution.py:69
  64.4 5.1 %collective-permute-start.5 = (bf16[192,512]{1,0:T(8,128)(2,1)S(1)}, bf16[192,512]{1,0:T(8,128)(2,1)S(1)}, u32[]{:S(2)}, u32[]{:S(2)}) collective-permute-start(bf16[192,512]{1,0:T(8,128)(2,1)S(1)} %collective-permute-done.3), channel_id=1, source_target_pairs={{0,480},{32,0},{64,32},{96,64},{128,96},{160,128},{192,160},{224,1... | collective-permute-start | bytes 589832 | tf_op jit(solution)/shard_map/ppermute | solution.py:72
  69.5 56.8 %collective-permute-start.6 = (bf16[192,512]{1,0:T(8,128)(2,1)S(1)}, bf16[192,512]{1,0:T(8,128)(2,1)S(1)}, u32[]{:S(2)}, u32[]{:S(2)}) collective-permute-start(bf16[192,512]{1,0:T(8,128)(2,1)S(1)} %collective-permute-done.4), channel_id=1, source_target_pairs={{0,32},{32,64},{64,96},{96,128},{128,160},{160,192},{192,224},{224... | collective-permute-start | bytes 589832 | tf_op jit(solution)/shard_map/ppermute | solution.py:69
  69.5 56.8 %collective-permute-start.7 = (bf16[192,512]{1,0:T(8,128)(2,1)S(1)}, bf16[192,512]{1,0:T(8,128)(2,1)S(1)}, u32[]{:S(2)}, u32[]{:S(2)}) collective-permute-start(bf16[192,512]{1,0:T(8,128)(2,1)S(1)} %collective-permute-done.5), channel_id=1, source_target_pairs={{0,480},{32,0},{64,32},{96,64},{128,96},{160,128},{192,160},{224,1... | collective-permute-start | bytes 589832 | tf_op jit(solution)/shard_map/ppermute | solution.py:72
  77.5 8.3 %collective-permute-start.15 = (bf16[6,512]{1,0:T(8,128)(2,1)S(1)}, bf16[6,512]{1,0:T(8,128)(2,1)S(1)}, u32[]{:S(2)}, u32[]{:S(2)}) collective-permute-start(bf16[6,512]{1,0:T(8,128)(2,1)S(1)} %subtract_convert_fusion), channel_id=1, source_target_pairs={{0,0},{1,32},{2,64},{3,96},{4,128},{5,160},{6,192},{7,224},{8,256}... | collective-permute-start | bytes 18440 | tf_op jit(solution)/shard_map/ppermute | solution.py:55
  105.2 24.2 %collective-permute-start.16 = (bf16[96,512]{1,0:T(8,128)(2,1)S(1)}, bf16[96,512]{1,0:T(8,128)(2,1)S(1)}, u32[]{:S(2)}, u32[]{:S(2)}) collective-permute-start(bf16[96,512]{1,0:T(8,128)(2,1)S(1)} %get-tuple-element.135), channel_id=1, source_target_pairs={{0,28},{4,0},{8,4},{12,8},{16,12},{20,16},{24,20},{28,24},{1,29},{... | collective-permute-start | bytes 294920 | tf_op jit(solution)/shard_map/ppermute | solution.py:87
  110.1 24.9 %collective-permute-start.19 = (bf16[96,512]{1,0:T(8,128)(2,1)S(1)}, bf16[96,512]{1,0:T(8,128)(2,1)S(1)}, u32[]{:S(2)}, u32[]{:S(2)}) collective-permute-start(bf16[96,512]{1,0:T(8,128)(2,1)S(1)} %get-tuple-element.135), channel_id=1, source_target_pairs={{0,4},{4,8},{8,12},{12,16},{16,20},{20,24},{24,28},{28,0},{1,5},{5... | collective-permute-start | bytes 294920 | tf_op jit(solution)/shard_map/ppermute | solution.py:84
  126.2 19.4 %collective-permute-start.8 = (bf16[192,512]{1,0:T(8,128)(2,1)S(1)}, bf16[192,512]{1,0:T(8,128)(2,1)S(1)}, u32[]{:S(2)}, u32[]{:S(2)}) collective-permute-start(bf16[192,512]{1,0:T(8,128)(2,1)S(1)} %collective-permute-done.6), channel_id=1, source_target_pairs={{0,32},{32,64},{64,96},{96,128},{128,160},{160,192},{192,224},{224... | collective-permute-start | bytes 589832 | tf_op jit(solution)/shard_map/ppermute | solution.py:69
  126.3 19.4 %collective-permute-start.9 = (bf16[192,512]{1,0:T(8,128)(2,1)S(1)}, bf16[192,512]{1,0:T(8,128)(2,1)S(1)}, u32[]{:S(2)}, u32[]{:S(2)}) collective-permute-start(bf16[192,512]{1,0:T(8,128)(2,1)S(1)} %collective-permute-done.7), channel_id=1, source_target_pairs={{0,480},{32,0},{64,32},{96,64},{128,96},{160,128},{192,160},{224,1... | collective-permute-start | bytes 589832 | tf_op jit(solution)/shard_map/ppermute | solution.py:72
  129.4 8.7 %collective-permute-start.17 = (bf16[96,512]{1,0:T(8,128)(2,1)S(1)}, bf16[96,512]{1,0:T(8,128)(2,1)S(1)}, u32[]{:S(2)}, u32[]{:S(2)}) collective-permute-start(bf16[96,512]{1,0:T(8,128)(2,1)S(1)} %collective-permute-done.16), channel_id=1, source_target_pairs={{0,28},{4,0},{8,4},{12,8},{16,12},{20,16},{24,20},{28,24},{1,29},{... | collective-permute-start | bytes 294920 | tf_op jit(solution)/shard_map/ppermute | solution.py:87
  135.0 8.7 %collective-permute-start.20 = (bf16[96,512]{1,0:T(8,128)(2,1)S(1)}, bf16[96,512]{1,0:T(8,128)(2,1)S(1)}, u32[]{:S(2)}, u32[]{:S(2)}) collective-permute-start(bf16[96,512]{1,0:T(8,128)(2,1)S(1)} %collective-permute-done.19), channel_id=1, source_target_pairs={{0,4},{4,8},{8,12},{12,16},{16,20},{20,24},{24,28},{28,0},{1,5},{5... | collective-permute-start | bytes 294920 | tf_op jit(solution)/shard_map/ppermute | solution.py:84
  138.1 18.0 %collective-permute-start.18 = (bf16[96,512]{1,0:T(8,128)(2,1)S(1)}, bf16[96,512]{1,0:T(8,128)(2,1)S(1)}, u32[]{:S(2)}, u32[]{:S(2)}) collective-permute-start(bf16[96,512]{1,0:T(8,128)(2,1)S(1)} %collective-permute-done.17), channel_id=1, source_target_pairs={{0,28},{4,0},{8,4},{12,8},{16,12},{20,16},{24,20},{28,24},{1,29},{... | collective-permute-start | bytes 294920 | tf_op jit(solution)/shard_map/ppermute | solution.py:87
  143.7 10.4 %collective-permute-start.21 = (bf16[96,512]{1,0:T(8,128)(2,1)S(1)}, bf16[96,512]{1,0:T(8,128)(2,1)S(1)}, u32[]{:S(2)}, u32[]{:S(2)}) collective-permute-start(bf16[96,512]{1,0:T(8,128)(2,1)S(1)} %collective-permute-done.20), channel_id=1, source_target_pairs={{0,4},{4,8},{8,12},{12,16},{16,20},{20,24},{24,28},{28,0},{1,5},{5... | collective-permute-start | bytes 294920 | tf_op jit(solution)/shard_map/ppermute | solution.py:84
  145.7 27.5 %collective-permute-start.10 = (bf16[192,512]{1,0:T(8,128)(2,1)S(1)}, bf16[192,512]{1,0:T(8,128)(2,1)S(1)}, u32[]{:S(2)}, u32[]{:S(2)}) collective-permute-start(bf16[192,512]{1,0:T(8,128)(2,1)S(1)} %collective-permute-done.8), channel_id=1, source_target_pairs={{0,32},{32,64},{64,96},{96,128},{128,160},{160,192},{192,224},{224... | collective-permute-start | bytes 589832 | tf_op jit(solution)/shard_map/ppermute | solution.py:69
  145.7 27.5 %collective-permute-start.11 = (bf16[192,512]{1,0:T(8,128)(2,1)S(1)}, bf16[192,512]{1,0:T(8,128)(2,1)S(1)}, u32[]{:S(2)}, u32[]{:S(2)}) collective-permute-start(bf16[192,512]{1,0:T(8,128)(2,1)S(1)} %collective-permute-done.9), channel_id=1, source_target_pairs={{0,480},{32,0},{64,32},{96,64},{128,96},{160,128},{192,160},{224,1... | collective-permute-start | bytes 589832 | tf_op jit(solution)/shard_map/ppermute | solution.py:72
  154.2 10.2 %collective-permute-start.22 = (bf16[96,512]{1,0:T(8,128)(2,1)S(1)}, bf16[96,512]{1,0:T(8,128)(2,1)S(1)}, u32[]{:S(2)}, u32[]{:S(2)}) collective-permute-start(bf16[96,512]{1,0:T(8,128)(2,1)S(1)} %collective-permute-done.21), channel_id=1, source_target_pairs={{0,4},{4,8},{8,12},{12,16},{16,20},{20,24},{24,28},{28,0},{1,5},{5... | collective-permute-start | bytes 294920 | tf_op jit(solution)/shard_map/ppermute | solution.py:84
  164.7 20.9 %collective-permute-start.24 = (bf16[8,96,512]{2,1,0:T(8,128)(2,1)S(1)}, bf16[8,96,512]{2,1,0:T(8,128)(2,1)S(1)}, u32[]{:S(2)}, u32[]{:S(2)}) collective-permute-start(bf16[8,96,512]{2,1,0:T(8,128)(2,1)S(1)} %get-tuple-element.129), channel_id=1, source_target_pairs={{0,1},{1,2},{2,3},{3,0},{4,5},{5,6},{6,7},{7,4},{8,9},{9,10},{10,1... | collective-permute-start | bytes 2359304 | tf_op jit(solution)/shard_map/ppermute | solution.py:84
  168.0 21.5 %collective-permute-start.23 = (bf16[8,96,512]{2,1,0:T(8,128)(2,1)S(1)}, bf16[8,96,512]{2,1,0:T(8,128)(2,1)S(1)}, u32[]{:S(2)}, u32[]{:S(2)}) collective-permute-start(bf16[8,96,512]{2,1,0:T(8,128)(2,1)S(1)} %get-tuple-element.129), channel_id=1, source_target_pairs={{0,3},{1,0},{2,1},{3,2},{4,7},{5,4},{6,5},{7,6},{8,11},{9,8},{10,9... | collective-permute-start | bytes 2359304 | tf_op jit(solution)/shard_map/ppermute | solution.py:87
  173.2 5.1 %collective-permute-start.12 = (bf16[192,512]{1,0:T(8,128)(2,1)S(1)}, bf16[192,512]{1,0:T(8,128)(2,1)S(1)}, u32[]{:S(2)}, u32[]{:S(2)}) collective-permute-start(bf16[192,512]{1,0:T(8,128)(2,1)S(1)} %collective-permute-done.10), channel_id=1, source_target_pairs={{0,32},{32,64},{64,96},{96,128},{128,160},{160,192},{192,224},{224... | collective-permute-start | bytes 589832 | tf_op jit(solution)/shard_map/ppermute | solution.py:69
  173.2 15.0 %collective-permute-start.13 = (bf16[192,512]{1,0:T(8,128)(2,1)S(1)}, bf16[192,512]{1,0:T(8,128)(2,1)S(1)}, u32[]{:S(2)}, u32[]{:S(2)}) collective-permute-start(bf16[192,512]{1,0:T(8,128)(2,1)S(1)} %collective-permute-done.11), channel_id=1, source_target_pairs={{0,480},{32,0},{64,32},{96,64},{128,96},{160,128},{192,160},{224,1... | collective-permute-start | bytes 589832 | tf_op jit(solution)/shard_map/ppermute | solution.py:72
  178.3 10.6 %collective-permute-start.14 = (bf16[192,512]{1,0:T(8,128)(2,1)S(1)}, bf16[192,512]{1,0:T(8,128)(2,1)S(1)}, u32[]{:S(2)}, u32[]{:S(2)}) collective-permute-start(bf16[192,512]{1,0:T(8,128)(2,1)S(1)} %collective-permute-done.12), channel_id=1, source_target_pairs={{0,32},{32,64},{64,96},{96,128},{128,160},{160,192},{192,224},{224... | collective-permute-start | bytes 589832 | tf_op jit(solution)/shard_map/ppermute | solution.py:69
  185.6 19.9 %collective-permute-start.25 = (bf16[8,96,512]{2,1,0:T(8,128)(2,1)S(1)}, bf16[8,96,512]{2,1,0:T(8,128)(2,1)S(1)}, u32[]{:S(2)}, u32[]{:S(2)}) collective-permute-start(bf16[8,96,512]{2,1,0:T(8,128)(2,1)S(1)} %collective-permute-done.24), channel_id=1, source_target_pairs={{0,1},{1,2},{2,3},{3,0},{4,5},{5,6},{6,7},{7,4},{8,9},{9,10},{10,1... | collective-permute-start | bytes 2359304 | tf_op jit(solution)/shard_map/ppermute | solution.py:84
  211.3 4.8 %copy-start.3 = (f32[512,512]{0,1:T(8,128)S(1)}, f32[512,512]{0,1:T(8,128)}, u32[]{:S(2)}) copy-start(f32[512,512]{0,1:T(8,128)} %fusion.19) | copy-start | bytes 3145732
Sparse Core Ops, SparseCore 0:
  126.3 52.9 all-gather.3
where the time goes:
time: 227 us; the launch traced here: 225 us
  starting transfers between devices  63.5 us (28%)
  waiting for transfers between devices  50.7 us (22%)
  blocking collectives  50.3 us (22%)
  local copies, waits for them, and re-layouts  30.4 us (13%)
  between operations  14.8 us (7%)
  matrix products  10.2 us (4%)
  other arithmetic  4.88 us (2%)
    ppermute x6, waiting for transfers between devices, ring_stage(): f = lax.ppermute(f, axis, fwd)  38.1 us
    ppermute x4, starting transfers between devices, ring_stage(): r = lax.ppermute(r, axis, bwd)  21.2 us
    all_gather x1, blocking collectives, route_errors(): return lax.all_gather(moved, 'tm', axis=0, tiled=True)  18.8 us
    all_gather x1, blocking collectives, shards(): ends = lax.all_gather(states[-1], 'tm', axis=0)  17.3 us
    all_gather x1, blocking collectives, weighted_gather(): first = lax.all_gather(weighted[:, :half], 'x', axis=0, tiled=True)  14.1 us
    ppermute x7, starting transfers between devices, ring_gather(): b = lax.ppermute(b, axis, bwd)  13.4 us
    dynamic_slice x16, local copies, waits for them, and re-layouts, step(): return jnp.where(k < a, span * carry + ends[k], carry)  11.7 us
    ppermute x6, starting transfers between devices, ring_stage(): f = lax.ppermute(f, axis, fwd)  11.5 us
  transfers between devices with their start and end apart: 28, of which 10 were waited for; matrix products, arithmetic and copies ran while one was open for 8% of the time, Pallas kernels for 0%

commit v1 on v0

--- a/solution.py
+++ b/solution.py
@@ -54,7 +54,9 @@
             perm.append((a * npre + b, dst_a * npre + dst_b))
     moved = lax.ppermute(errors, ("tm",) + PRE, perm)
     assert per == ntm
-    return lax.all_gather(moved, "tm", axis=0, tiled=True)
+    return jnp.concatenate(
+        lax.all_to_all(jnp.stack([moved] * lax.axis_size("tm")), "tm", 0, 0), axis=0
+    )
 
 
 def ring_gather(block, axis, count):

time: 227 us -> 225 us (level)
  the two profiles are of different devices: /device:TPU:16 before, /device:TPU:56 now
where the time goes in v1:
time: 225 us; the launch traced here: 223 us
  starting transfers between devices  68.9 us (31%)
  waiting for transfers between devices  57.7 us (26%)
  blocking collectives  33.6 us (15%)
  local copies, waits for them, and re-layouts  32.9 us (15%)
  between operations  14.8 us (7%)
  matrix products  10.2 us (5%)
  other arithmetic  4.87 us (2%)
    ppermute x6, waiting for transfers between devices, ring_stage(): f = lax.ppermute(f, axis, fwd)  40.6 us
    ppermute x4, starting transfers between devices, ring_stage(): r = lax.ppermute(r, axis, bwd)  19 us
    all_gather x1, blocking collectives, shards(): ends = lax.all_gather(states[-1], 'tm', axis=0)  18.1 us
    all_gather x1, blocking collectives, weighted_gather(): first = lax.all_gather(weighted[:, :half], 'x', axis=0, tiled=True)  15.4 us
    ppermute x6, starting transfers between devices, ring_stage(): f = lax.ppermute(f, axis, fwd)  11.9 us
    dynamic_slice x16, local copies, waits for them, and re-layouts, step(): return jnp.where(k < a, span * carry + ends[k], carry)  11.7 us
    all_to_all x1, starting transfers between devices, owned_errors(): pieces = lax.all_to_all(partial_logits, PRE, 0, 0, tiled=True)  10.2 us
    dot_general x2, matrix products, outer_sum(): lax.dot_general(left_rows, right_rows, (((0,), (0,)), ((), ())), preferre...  9.45 us
  transfers between devices with their start and end apart: 29, of which 12 were waited for; matrix products, arithmetic and copies ran while one was open for 9% of the time, Pallas kernels for 0%

profile of v1, /device:TPU:56, one launch (start us, length us, event | category | flops | bytes accessed | tf_op | source)
XLA Modules:
  0.0 223.1 jit_solution(4324637915396537435)
XLA Ops:
  6.5 0.8 broadcast_subtract_fusion
  7.3 1.0 convert_multiply_fusion
  8.6 0.7 multiply_add_fusion
  11.6 18.1 %all-gather = f32[16,1,512]{2,1,0:T(1,128)S(1)} all-gather(f32[1,1,512]{2,1,0:T(1,128)S(1)} %add_bitcast_fusion), channel_id=1, replica_groups=mesh['tm'=16,'z'=8,'x'=4] {'tm'}, dimensions={0}, use_global_device_ids=true | all-gather | bytes 34816 | tf_op jit(solution)/shard_map/all_gather | solution.py:123
  30.5 12.1 %while.14 = (s32[]{:T(128)}, f32[512]{0:T(512)S(1)}, s32[]{:T(128)}, f32[512]{0:T(512)S(1)}, f32[16,512]{1,0:T(8,128)}, /*index=5*/s32[]{:T(128)}, s32[]{:T(128)}) while((s32[]{:T(128)}, f32[512]{0:T(512)S(1)}, s32[]{:T(128)}, f32[512]{0:T(512)S(1)}, f32[16,512]{1,0:T(8,128)}, /*index=5*/s32[]{:T(128)}, s32[]{:T(128)}) %tuple.58), condition=%wide.region_1.0_spmd.clone, body=%wide.region_0.0_spmd.clone.sunk | while | flops 2052 | bytes 12389 | solution.py:129
  30.6 0.8 constant_dynamic-slice_fusion.4
  31.4 0.7 constant_dynamic-slice_fusion.4
  32.1 0.7 constant_dynamic-slice_fusion.4
  32.9 0.7 constant_dynamic-slice_fusion.4
  33.6 0.7 constant_dynamic-slice_fusion.4
  34.4 0.7 constant_dynamic-slice_fusion.4
  35.1 0.7 constant_dynamic-slice_fusion.4
  35.9 0.7 constant_dynamic-slice_fusion.4
  36.6 0.7 constant_dynamic-slice_fusion.4
  37.4 0.7 constant_dynamic-slice_fusion.4
  38.1 0.7 constant_dynamic-slice_fusion.4
  38.9 0.7 constant_dynamic-slice_fusion.4
  39.6 0.7 constant_dynamic-slice_fusion.4
  40.4 0.7 constant_dynamic-slice_fusion.4
  41.1 0.7 constant_dynamic-slice_fusion.4
  41.9 0.7 constant_dynamic-slice_fusion.4
  42.6 2.0 broadcast_in_dim.65
  44.6 0.9 bitcast_dynamic-update-slice_fusion.23
  45.9 1.4 collective-permute-start.1
  47.5 0.8 all_to_all.9
  48.4 10.2 %all-to-all-start = ((f32[32,6,512]{2,1,0:T(8,128)}), f32[32,6,512]{2,1,0:T(8,128)S(1)}, u32[]{:S(2)}, u32[]{:S(2)}) async-start(f32[32,6,512]{2,1,0:T(8,128)} %all_to_all.9), calls=%async_computation | async-start | bytes 1048576 | tf_op jit(solution)/shard_map/all_to_all | solution.py:35
  59.5 1.2 collective-permute-start.3
  61.4 0.7 bitcast_dynamic-update-slice_fusion.21
  62.1 2.0 collective-permute-done.2
  64.1 1.3 collective-permute-start.4
  67.2 2.0 collective-permute-done.4
  69.2 2.5 %collective-permute-start.6 = (bf16[192,512]{1,0:T(8,128)(2,1)S(1)}, bf16[192,512]{1,0:T(8,128)(2,1)}, u32[]{:S(2)}, u32[]{:S(2)}) collective-permute-start(bf16[192,512]{1,0:T(8,128)(2,1)S(1)} %collective-permute-done.4), channel_id=1, source_target_pairs={{0,32},{32,64},{64,96},{96,128},{128,160},{160,192},{192,224},{224... | collective-permute-start | bytes 589832 | tf_op jit(solution)/shard_map/ppermute | solution.py:71
  71.7 0.7 bitcast_dynamic-update-slice_fusion.18
  72.4 4.4 %all-to-all-done = f32[32,6,512]{2,1,0:T(8,128)S(1)} async-done(((f32[32,6,512]{2,1,0:T(8,128)}), f32[32,6,512]{2,1,0:T(8,128)S(1)}, u32[]{:S(2)}, u32[]{:S(2)}) %all-to-all-start) | async-done | bytes 393248 | tf_op jit(solution)/shard_map/all_to_all | solution.py:35
  77.3 6.8 %collective-permute-start.15 = (bf16[6,512]{1,0:T(8,128)(2,1)S(1)}, bf16[6,512]{1,0:T(8,128)(2,1)S(1)}, u32[]{:S(2)}, u32[]{:S(2)}) collective-permute-start(bf16[6,512]{1,0:T(8,128)(2,1)S(1)} %subtract_convert_fusion), channel_id=1, source_target_pairs={{0,0},{1,32},{2,64},{3,96},{4,128},{5,160},{6,192},{7,224},{8,256}... | collective-permute-start | bytes 18440 | tf_op jit(solution)/shard_map/ppermute | solution.py:55
  84.8 4.4 %collective-permute-done.15 = bf16[6,512]{1,0:T(8,128)(2,1)S(1)} collective-permute-done((bf16[6,512]{1,0:T(8,128)(2,1)S(1)}, bf16[6,512]{1,0:T(8,128)(2,1)S(1)}, u32[]{:S(2)}, u32[]{:S(2)}) %collective-permute-start.15) | collective-permute-done | bytes 6176 | tf_op jit(solution)/shard_map/ppermute | solution.py:55
  89.8 7.7 %all-to-all-start.1 = ((bf16[16,6,512]{2,1,0:T(8,128)(2,1)}), bf16[16,6,512]{2,1,0:T(8,128)(2,1)S(1)}, u32[]{:S(2)}, u32[]{:S(2)}) async-start(bf16[16,6,512]{2,1,0:T(8,128)(2,1)} %stack.30), calls=%async_computation.1 | async-start | bytes 262144 | tf_op jit(solution)/shard_map/all_to_all | solution.py:58
  97.7 1.6 collective-permute-start.9
  99.3 1.6 bitcast_dynamic-update-slice_fusion.16
  100.9 1.6 bitcast_dynamic-update-slice_fusion.15
  102.6 0.7 all-to-all-done.1
  103.8 3.5 %collective-permute-start.16 = (bf16[96,512]{1,0:T(8,128)(2,1)S(1)}, bf16[96,512]{1,0:T(8,128)(2,1)S(1)}, u32[]{:S(2)}, u32[]{:S(2)}) collective-permute-start(bf16[96,512]{1,0:T(8,128)(2,1)S(1)} %get-tuple-element.135), channel_id=1, source_target_pairs={{0,28},{4,0},{8,4},{12,8},{16,12},{20,16},{24,20},{28,24},{1,29},{... | collective-permute-start | bytes 294920 | tf_op jit(solution)/shard_map/ppermute | solution.py:89
  107.3 2.4 %collective-permute-start.19 = (bf16[96,512]{1,0:T(8,128)(2,1)S(1)}, bf16[96,512]{1,0:T(8,128)(2,1)S(1)}, u32[]{:S(2)}, u32[]{:S(2)}) collective-permute-start(bf16[96,512]{1,0:T(8,128)(2,1)S(1)} %get-tuple-element.135), channel_id=1, source_target_pairs={{0,4},{4,8},{8,12},{12,16},{16,20},{20,24},{24,28},{28,0},{1,5},{5... | collective-permute-start | bytes 294920 | tf_op jit(solution)/shard_map/ppermute | solution.py:86
  109.7 15.4 %all_gather.10 = bf16[384,512]{1,0:T(8,128)(2,1)} all-gather(bf16[96,512]{1,0:T(8,128)(2,1)S(1)} %get-tuple-element.134), channel_id=1, replica_groups=mesh['tm'=16,'z'=8,'x'=4] {'x'}, dimensions={0}, use_global_device_ids=true | all-gather | bytes 491520 | tf_op jit(solution)/shard_map/all_gather | solution.py:100
  125.2 1.7 collective-permute-start.11
  126.9 4.9 %collective-permute-start.17 = (bf16[96,512]{1,0:T(8,128)(2,1)S(1)}, bf16[96,512]{1,0:T(8,128)(2,1)S(1)}, u32[]{:S(2)}, u32[]{:S(2)}) collective-permute-start(bf16[96,512]{1,0:T(8,128)(2,1)S(1)} %collective-permute-done.16), channel_id=1, source_target_pairs={{0,28},{4,0},{8,4},{12,8},{16,12},{20,16},{24,20},{28,24},{1,29},{... | collective-permute-start | bytes 294920 | tf_op jit(solution)/shard_map/ppermute | solution.py:89
  131.8 1.9 collective-permute-start.20
  133.7 0.9 collective-permute-done.17
  134.7 5.6 %collective-permute-start.18 = (bf16[96,512]{1,0:T(8,128)(2,1)S(1)}, bf16[96,512]{1,0:T(8,128)(2,1)S(1)}, u32[]{:S(2)}, u32[]{:S(2)}) collective-permute-start(bf16[96,512]{1,0:T(8,128)(2,1)S(1)} %collective-permute-done.17), channel_id=1, source_target_pairs={{0,28},{4,0},{8,4},{12,8},{16,12},{20,16},{24,20},{28,24},{1,29},{... | collective-permute-start | bytes 294920 | tf_op jit(solution)/shard_map/ppermute | solution.py:89
  140.6 1.9 collective-permute-start.21
  142.5 8.6 %collective-permute-done.21 = bf16[96,512]{1,0:T(8,128)(2,1)S(1)} collective-permute-done((bf16[96,512]{1,0:T(8,128)(2,1)S(1)}, bf16[96,512]{1,0:T(8,128)(2,1)S(1)}, u32[]{:S(2)}, u32[]{:S(2)}) %collective-permute-start.21) | collective-permute-done | bytes 98336 | tf_op jit(solution)/shard_map/ppermute | solution.py:86
  151.1 1.9 collective-permute-start.22
  153.0 8.0 %collective-permute-done.22 = bf16[96,512]{1,0:T(8,128)(2,1)S(1)} collective-permute-done((bf16[96,512]{1,0:T(8,128)(2,1)S(1)}, bf16[96,512]{1,0:T(8,128)(2,1)S(1)}, u32[]{:S(2)}, u32[]{:S(2)}) %collective-permute-start.22) | collective-permute-done | bytes 98336 | tf_op jit(solution)/shard_map/ppermute | solution.py:86
  161.5 1.9 collective-permute-start.24
  164.8 1.7 collective-permute-start.13
  166.5 0.7 bitcast_dynamic-update-slice_fusion.12
  167.2 5.1 %collective-permute-start.23 = (bf16[8,96,512]{2,1,0:T(8,128)(2,1)S(1)}, bf16[8,96,512]{2,1,0:T(8,128)(2,1)S(1)}, u32[]{:S(2)}, u32[]{:S(2)}) collective-permute-start(bf16[8,96,512]{2,1,0:T(8,128)(2,1)S(1)} %get-tuple-element.129), channel_id=1, source_target_pairs={{0,3},{1,0},{2,1},{3,2},{4,7},{5,4},{6,5},{7,6},{8,11},{9,8},{10,9... | collective-permute-start | bytes 2359304 | tf_op jit(solution)/shard_map/ppermute | solution.py:89
  173.2 9.8 %collective-permute-done.24 = bf16[8,96,512]{2,1,0:T(8,128)(2,1)S(1)} collective-permute-done((bf16[8,96,512]{2,1,0:T(8,128)(2,1)S(1)}, bf16[8,96,512]{2,1,0:T(8,128)(2,1)S(1)}, u32[]{:S(2)}, u32[]{:S(2)}) %collective-permute-start.24) | collective-permute-done | bytes 786464 | tf_op jit(solution)/shard_map/ppermute | solution.py:86
  183.0 1.9 collective-permute-start.25
  187.1 2.7 %collective-permute-done.23 = bf16[8,96,512]{2,1,0:T(8,128)(2,1)S(1)} collective-permute-done((bf16[8,96,512]{2,1,0:T(8,128)(2,1)S(1)}, bf16[8,96,512]{2,1,0:T(8,128)(2,1)S(1)}, u32[]{:S(2)}, u32[]{:S(2)}) %collective-permute-start.23) | collective-permute-done | bytes 786464 | tf_op jit(solution)/shard_map/ppermute | solution.py:89
  189.8 13.9 %collective-permute-done.25 = bf16[8,96,512]{2,1,0:T(8,128)(2,1)S(1)} collective-permute-done((bf16[8,96,512]{2,1,0:T(8,128)(2,1)S(1)}, bf16[8,96,512]{2,1,0:T(8,128)(2,1)S(1)}, u32[]{:S(2)}, u32[]{:S(2)}) %collective-permute-start.25) | collective-permute-done | bytes 786464 | tf_op jit(solution)/shard_map/ppermute | solution.py:86
  204.8 4.7 %fusion.19 = f32[512,512]{0,1:T(8,128)} fusion(bf16[3072,512]{1,0:T(8,128)(2,1)} %bitcast.27, bf16[3072,512]{1,0:T(8,128)(2,1)S(1)} %bitcast.97), kind=kOutput, calls=%fused_computation.114 | convolution fusion | flops 1610612736 | bytes 7340032 | tf_op jit(solution)/shard_map/dot_general | solution.py:138
  209.5 4.8 %fusion.18 = f32[512,512]{0,1:T(8,128)S(1)} fusion(bf16[3072,512]{1,0:T(8,128)(2,1)} %bitcast.27, bf16[3072,512]{1,0:T(8,128)(2,1)} %all-gather.3.cloned.1.call-done), kind=kOutput, calls=%fused_computation.113 | convolution fusion | flops 1610612736 | bytes 7340032 | tf_op jit(solution)/shard_map/dot_general | solution.py:138
  214.4 1.8 copy.11
  (199 shorter events, 15.5 us)
Async XLA Ops:
  6.5 96.8 %copy-start = (bf16[1024,512]{1,0:T(8,128)(2,1)S(1)}, bf16[1024,512]{1,0:T(8,128)(2,1)}, u32[]{:S(2)}) copy-start(bf16[1024,512]{1,0:T(8,128)(2,1)} %param.12) | copy-start | bytes 3145732
  8.4 2.4 %copy-start.1 = (f32[192,512]{1,0:T(8,128)}, f32[192,512]{1,0:T(8,128)S(1)}, u32[]{:S(2)}) copy-start(f32[192,512]{1,0:T(8,128)S(1)} %convert_multiply_fusion) | copy-start | bytes 1179652
  10.6 0.7 copy-start.6
  10.8 0.7 slice-start
  30.4 16.9 %copy-start.2 = (s32[192,512]{1,0:T(8,128)S(1)}, s32[192,512]{1,0:T(8,128)}, u32[]{:S(2)}) copy-start(s32[192,512]{1,0:T(8,128)} %param.8) | copy-start | bytes 1179652
  30.5 16.8 %copy-start.4 = (bf16[512,512]{1,0:T(8,128)(2,1)S(1)}, bf16[512,512]{1,0:T(8,128)(2,1)}, u32[]{:S(2)}) copy-start(bf16[512,512]{1,0:T(8,128)(2,1)} %param.11) | copy-start | bytes 1572868
  44.6 14.3 %copy-start.7 = (s32[192]{0:T(256)S(1)}, s32[192]{0:T(256)}, u32[]{:S(2)}) copy-start(s32[192]{0:T(256)} %param.13) | copy-start | bytes 2308
  45.5 13.5 %collective-permute-start = (bf16[192,512]{1,0:T(8,128)(2,1)}, bf16[192,512]{1,0:T(8,128)(2,1)S(1)}, u32[]{:S(2)}, u32[]{:S(2)}) collective-permute-start(bf16[192,512]{1,0:T(8,128)(2,1)} %get-tuple-element.131), channel_id=1, source_target_pairs={{0,32},{32,64},{64,96},{96,128},{128,160},{160,192},{192,224},{224... | collective-permute-start | bytes 589832 | tf_op jit(solution)/shard_map/ppermute | solution.py:71
  45.9 13.7 %collective-permute-start.1 = (bf16[192,512]{1,0:T(8,128)(2,1)}, bf16[192,512]{1,0:T(8,128)(2,1)S(1)}, u32[]{:S(2)}, u32[]{:S(2)}) collective-permute-start(bf16[192,512]{1,0:T(8,128)(2,1)} %get-tuple-element.131), channel_id=1, source_target_pairs={{0,480},{32,0},{64,32},{96,64},{128,96},{160,128},{192,160},{224,1... | collective-permute-start | bytes 589832 | tf_op jit(solution)/shard_map/ppermute | solution.py:74
  48.4 54.9 %copy-start.5 = (bf16[96,1024]{1,0:T(8,128)(2,1)S(1)}, bf16[96,1024]{1,0:T(8,128)(2,1)}, u32[]{:S(2)}) copy-start(bf16[96,1024]{1,0:T(8,128)(2,1)} %param.10) | copy-start | bytes 589828
  48.4 28.4 %all-to-all-start = ((f32[32,6,512]{2,1,0:T(8,128)}), f32[32,6,512]{2,1,0:T(8,128)S(1)}, u32[]{:S(2)}, u32[]{:S(2)}) async-start(f32[32,6,512]{2,1,0:T(8,128)} %all_to_all.9), calls=%async_computation | async-start | bytes 1048576 | tf_op jit(solution)/shard_map/all_to_all | solution.py:35
  59.0 5.1 %collective-permute-start.2 = (bf16[192,512]{1,0:T(8,128)(2,1)S(1)}, bf16[192,512]{1,0:T(8,128)(2,1)S(1)}, u32[]{:S(2)}, u32[]{:S(2)}) collective-permute-start(bf16[192,512]{1,0:T(8,128)(2,1)S(1)} %collective-permute-done), channel_id=1, source_target_pairs={{0,32},{32,64},{64,96},{96,128},{128,160},{160,192},{192,224},{224... | collective-permute-start | bytes 589832 | tf_op jit(solution)/shard_map/ppermute | solution.py:71
  59.5 5.8 %collective-permute-start.3 = (bf16[192,512]{1,0:T(8,128)(2,1)S(1)}, bf16[192,512]{1,0:T(8,128)(2,1)S(1)}, u32[]{:S(2)}, u32[]{:S(2)}) collective-permute-start(bf16[192,512]{1,0:T(8,128)(2,1)S(1)} %collective-permute-done.1), channel_id=1, source_target_pairs={{0,480},{32,0},{64,32},{96,64},{128,96},{160,128},{192,160},{224,1... | collective-permute-start | bytes 589832 | tf_op jit(solution)/shard_map/ppermute | solution.py:74
  64.1 5.1 %collective-permute-start.4 = (bf16[192,512]{1,0:T(8,128)(2,1)S(1)}, bf16[192,512]{1,0:T(8,128)(2,1)S(1)}, u32[]{:S(2)}, u32[]{:S(2)}) collective-permute-start(bf16[192,512]{1,0:T(8,128)(2,1)S(1)} %collective-permute-done.2), channel_id=1, source_target_pairs={{0,32},{32,64},{64,96},{96,128},{128,160},{160,192},{192,224},{224... | collective-permute-start | bytes 589832 | tf_op jit(solution)/shard_map/ppermute | solution.py:71
  65.4 6.3 %collective-permute-start.5 = (bf16[192,512]{1,0:T(8,128)(2,1)S(1)}, bf16[192,512]{1,0:T(8,128)(2,1)S(1)}, u32[]{:S(2)}, u32[]{:S(2)}) collective-permute-start(bf16[192,512]{1,0:T(8,128)(2,1)S(1)} %collective-permute-done.3), channel_id=1, source_target_pairs={{0,480},{32,0},{64,32},{96,64},{128,96},{160,128},{192,160},{224,1... | collective-permute-start | bytes 589832 | tf_op jit(solution)/shard_map/ppermute | solution.py:74
  69.2 28.4 %collective-permute-start.6 = (bf16[192,512]{1,0:T(8,128)(2,1)S(1)}, bf16[192,512]{1,0:T(8,128)(2,1)}, u32[]{:S(2)}, u32[]{:S(2)}) collective-permute-start(bf16[192,512]{1,0:T(8,128)(2,1)S(1)} %collective-permute-done.4), channel_id=1, source_target_pairs={{0,32},{32,64},{64,96},{96,128},{128,160},{160,192},{192,224},{224... | collective-permute-start | bytes 589832 | tf_op jit(solution)/shard_map/ppermute | solution.py:71
  71.7 26.0 %collective-permute-start.7 = (bf16[192,512]{1,0:T(8,128)(2,1)S(1)}, bf16[192,512]{1,0:T(8,128)(2,1)}, u32[]{:S(2)}, u32[]{:S(2)}) collective-permute-start(bf16[192,512]{1,0:T(8,128)(2,1)S(1)} %collective-permute-done.5), channel_id=1, source_target_pairs={{0,480},{32,0},{64,32},{96,64},{128,96},{160,128},{192,160},{224,1... | collective-permute-start | bytes 589832 | tf_op jit(solution)/shard_map/ppermute | solution.py:74
  77.3 11.9 %collective-permute-start.15 = (bf16[6,512]{1,0:T(8,128)(2,1)S(1)}, bf16[6,512]{1,0:T(8,128)(2,1)S(1)}, u32[]{:S(2)}, u32[]{:S(2)}) collective-permute-start(bf16[6,512]{1,0:T(8,128)(2,1)S(1)} %subtract_convert_fusion), channel_id=1, source_target_pairs={{0,0},{1,32},{2,64},{3,96},{4,128},{5,160},{6,192},{7,224},{8,256}... | collective-permute-start | bytes 18440 | tf_op jit(solution)/shard_map/ppermute | solution.py:55
  89.8 13.5 %all-to-all-start.1 = ((bf16[16,6,512]{2,1,0:T(8,128)(2,1)}), bf16[16,6,512]{2,1,0:T(8,128)(2,1)S(1)}, u32[]{:S(2)}, u32[]{:S(2)}) async-start(bf16[16,6,512]{2,1,0:T(8,128)(2,1)} %stack.30), calls=%async_computation.1 | async-start | bytes 262144 | tf_op jit(solution)/shard_map/all_to_all | solution.py:58
  97.5 112.0 %all-gather.3.cloned.1.call-start = ((), (), s32[]{:S(2)}) async-start(), calls=%async_computation.2 | async-start | bytes 3538944 | tf_op jit(solution)/shard_map/all_gather | solution.py:101
  97.6 27.6 %collective-permute-start.8 = (bf16[192,512]{1,0:T(8,128)(2,1)}, bf16[192,512]{1,0:T(8,128)(2,1)S(1)}, u32[]{:S(2)}, u32[]{:S(2)}) collective-permute-start(bf16[192,512]{1,0:T(8,128)(2,1)} %collective-permute-done.6), channel_id=1, source_target_pairs={{0,32},{32,64},{64,96},{96,128},{128,160},{160,192},{192,224},{224... | collective-permute-start | bytes 589832 | tf_op jit(solution)/shard_map/ppermute | solution.py:71
  97.7 27.5 %collective-permute-start.9 = (bf16[192,512]{1,0:T(8,128)(2,1)}, bf16[192,512]{1,0:T(8,128)(2,1)S(1)}, u32[]{:S(2)}, u32[]{:S(2)}) collective-permute-start(bf16[192,512]{1,0:T(8,128)(2,1)} %collective-permute-done.7), channel_id=1, source_target_pairs={{0,480},{32,0},{64,32},{96,64},{128,96},{160,128},{192,160},{224,1... | collective-permute-start | bytes 589832 | tf_op jit(solution)/shard_map/ppermute | solution.py:74
  103.8 23.1 %collective-permute-start.16 = (bf16[96,512]{1,0:T(8,128)(2,1)S(1)}, bf16[96,512]{1,0:T(8,128)(2,1)S(1)}, u32[]{:S(2)}, u32[]{:S(2)}) collective-permute-start(bf16[96,512]{1,0:T(8,128)(2,1)S(1)} %get-tuple-element.135), channel_id=1, source_target_pairs={{0,28},{4,0},{8,4},{12,8},{16,12},{20,16},{24,20},{28,24},{1,29},{... | collective-permute-start | bytes 294920 | tf_op jit(solution)/shard_map/ppermute | solution.py:89
  107.3 24.5 %collective-permute-start.19 = (bf16[96,512]{1,0:T(8,128)(2,1)S(1)}, bf16[96,512]{1,0:T(8,128)(2,1)S(1)}, u32[]{:S(2)}, u32[]{:S(2)}) collective-permute-start(bf16[96,512]{1,0:T(8,128)(2,1)S(1)} %get-tuple-element.135), channel_id=1, source_target_pairs={{0,4},{4,8},{8,12},{12,16},{16,20},{20,24},{24,28},{28,0},{1,5},{5... | collective-permute-start | bytes 294920 | tf_op jit(solution)/shard_map/ppermute | solution.py:86
  125.2 39.6 %collective-permute-start.10 = (bf16[192,512]{1,0:T(8,128)(2,1)S(1)}, bf16[192,512]{1,0:T(8,128)(2,1)S(1)}, u32[]{:S(2)}, u32[]{:S(2)}) collective-permute-start(bf16[192,512]{1,0:T(8,128)(2,1)S(1)} %collective-permute-done.8), channel_id=1, source_target_pairs={{0,32},{32,64},{64,96},{96,128},{128,160},{160,192},{192,224},{224... | collective-permute-start | bytes 589832 | tf_op jit(solution)/shard_map/ppermute | solution.py:71
  125.2 39.6 %collective-permute-start.11 = (bf16[192,512]{1,0:T(8,128)(2,1)S(1)}, bf16[192,512]{1,0:T(8,128)(2,1)S(1)}, u32[]{:S(2)}, u32[]{:S(2)}) collective-permute-start(bf16[192,512]{1,0:T(8,128)(2,1)S(1)} %collective-permute-done.9), channel_id=1, source_target_pairs={{0,480},{32,0},{64,32},{96,64},{128,96},{160,128},{192,160},{224,1... | collective-permute-start | bytes 589832 | tf_op jit(solution)/shard_map/ppermute | solution.py:74
  126.9 7.8 %collective-permute-start.17 = (bf16[96,512]{1,0:T(8,128)(2,1)S(1)}, bf16[96,512]{1,0:T(8,128)(2,1)S(1)}, u32[]{:S(2)}, u32[]{:S(2)}) collective-permute-start(bf16[96,512]{1,0:T(8,128)(2,1)S(1)} %collective-permute-done.16), channel_id=1, source_target_pairs={{0,28},{4,0},{8,4},{12,8},{16,12},{20,16},{24,20},{28,24},{1,29},{... | collective-permute-start | bytes 294920 | tf_op jit(solution)/shard_map/ppermute | solution.py:89
  131.8 8.8 %collective-permute-start.20 = (bf16[96,512]{1,0:T(8,128)(2,1)S(1)}, bf16[96,512]{1,0:T(8,128)(2,1)S(1)}, u32[]{:S(2)}, u32[]{:S(2)}) collective-permute-start(bf16[96,512]{1,0:T(8,128)(2,1)S(1)} %collective-permute-done.19), channel_id=1, source_target_pairs={{0,4},{4,8},{8,12},{12,16},{16,20},{20,24},{24,28},{28,0},{1,5},{5... | collective-permute-start | bytes 294920 | tf_op jit(solution)/shard_map/ppermute | solution.py:86
  134.7 18.3 %collective-permute-start.18 = (bf16[96,512]{1,0:T(8,128)(2,1)S(1)}, bf16[96,512]{1,0:T(8,128)(2,1)S(1)}, u32[]{:S(2)}, u32[]{:S(2)}) collective-permute-start(bf16[96,512]{1,0:T(8,128)(2,1)S(1)} %collective-permute-done.17), channel_id=1, source_target_pairs={{0,28},{4,0},{8,4},{12,8},{16,12},{20,16},{24,20},{28,24},{1,29},{... | collective-permute-start | bytes 294920 | tf_op jit(solution)/shard_map/ppermute | solution.py:89
  140.6 10.5 %collective-permute-start.21 = (bf16[96,512]{1,0:T(8,128)(2,1)S(1)}, bf16[96,512]{1,0:T(8,128)(2,1)S(1)}, u32[]{:S(2)}, u32[]{:S(2)}) collective-permute-start(bf16[96,512]{1,0:T(8,128)(2,1)S(1)} %collective-permute-done.20), channel_id=1, source_target_pairs={{0,4},{4,8},{8,12},{12,16},{16,20},{20,24},{24,28},{28,0},{1,5},{5... | collective-permute-start | bytes 294920 | tf_op jit(solution)/shard_map/ppermute | solution.py:86
  151.1 10.0 %collective-permute-start.22 = (bf16[96,512]{1,0:T(8,128)(2,1)S(1)}, bf16[96,512]{1,0:T(8,128)(2,1)S(1)}, u32[]{:S(2)}, u32[]{:S(2)}) collective-permute-start(bf16[96,512]{1,0:T(8,128)(2,1)S(1)} %collective-permute-done.21), channel_id=1, source_target_pairs={{0,4},{4,8},{8,12},{12,16},{16,20},{20,24},{24,28},{28,0},{1,5},{5... | collective-permute-start | bytes 294920 | tf_op jit(solution)/shard_map/ppermute | solution.py:86
  161.5 21.6 %collective-permute-start.24 = (bf16[8,96,512]{2,1,0:T(8,128)(2,1)S(1)}, bf16[8,96,512]{2,1,0:T(8,128)(2,1)S(1)}, u32[]{:S(2)}, u32[]{:S(2)}) collective-permute-start(bf16[8,96,512]{2,1,0:T(8,128)(2,1)S(1)} %get-tuple-element.129), channel_id=1, source_target_pairs={{0,1},{1,2},{2,3},{3,0},{4,5},{5,6},{6,7},{7,4},{8,9},{9,10},{10,1... | collective-permute-start | bytes 2359304 | tf_op jit(solution)/shard_map/ppermute | solution.py:86
  164.8 8.3 %collective-permute-start.12 = (bf16[192,512]{1,0:T(8,128)(2,1)S(1)}, bf16[192,512]{1,0:T(8,128)(2,1)S(1)}, u32[]{:S(2)}, u32[]{:S(2)}) collective-permute-start(bf16[192,512]{1,0:T(8,128)(2,1)S(1)} %collective-permute-done.10), channel_id=1, source_target_pairs={{0,32},{32,64},{64,96},{96,128},{128,160},{160,192},{192,224},{224... | collective-permute-start | bytes 589832 | tf_op jit(solution)/shard_map/ppermute | solution.py:71
  164.8 20.9 %collective-permute-start.13 = (bf16[192,512]{1,0:T(8,128)(2,1)S(1)}, bf16[192,512]{1,0:T(8,128)(2,1)S(1)}, u32[]{:S(2)}, u32[]{:S(2)}) collective-permute-start(bf16[192,512]{1,0:T(8,128)(2,1)S(1)} %collective-permute-done.11), channel_id=1, source_target_pairs={{0,480},{32,0},{64,32},{96,64},{128,96},{160,128},{192,160},{224,1... | collective-permute-start | bytes 589832 | tf_op jit(solution)/shard_map/ppermute | solution.py:74
  167.2 22.5 %collective-permute-start.23 = (bf16[8,96,512]{2,1,0:T(8,128)(2,1)S(1)}, bf16[8,96,512]{2,1,0:T(8,128)(2,1)S(1)}, u32[]{:S(2)}, u32[]{:S(2)}) collective-permute-start(bf16[8,96,512]{2,1,0:T(8,128)(2,1)S(1)} %get-tuple-element.129), channel_id=1, source_target_pairs={{0,3},{1,0},{2,1},{3,2},{4,7},{5,4},{6,5},{7,6},{8,11},{9,8},{10,9... | collective-permute-start | bytes 2359304 | tf_op jit(solution)/shard_map/ppermute | solution.py:89
  173.0 13.3 %collective-permute-start.14 = (bf16[192,512]{1,0:T(8,128)(2,1)S(1)}, bf16[192,512]{1,0:T(8,128)(2,1)S(1)}, u32[]{:S(2)}, u32[]{:S(2)}) collective-permute-start(bf16[192,512]{1,0:T(8,128)(2,1)S(1)} %collective-permute-done.12), channel_id=1, source_target_pairs={{0,32},{32,64},{64,96},{96,128},{128,160},{160,192},{192,224},{224... | collective-permute-start | bytes 589832 | tf_op jit(solution)/shard_map/ppermute | solution.py:71
  183.0 20.7 %collective-permute-start.25 = (bf16[8,96,512]{2,1,0:T(8,128)(2,1)S(1)}, bf16[8,96,512]{2,1,0:T(8,128)(2,1)S(1)}, u32[]{:S(2)}, u32[]{:S(2)}) collective-permute-start(bf16[8,96,512]{2,1,0:T(8,128)(2,1)S(1)} %collective-permute-done.24), channel_id=1, source_target_pairs={{0,1},{1,2},{2,3},{3,0},{4,5},{5,6},{6,7},{7,4},{8,9},{9,10},{10,1... | collective-permute-start | bytes 2359304 | tf_op jit(solution)/shard_map/ppermute | solution.py:86
  209.5 4.8 %copy-start.3 = (f32[512,512]{0,1:T(8,128)S(1)}, f32[512,512]{0,1:T(8,128)}, u32[]{:S(2)}) copy-start(f32[512,512]{0,1:T(8,128)} %fusion.19) | copy-start | bytes 3145732
Sparse Core Ops, SparseCore 0:
  125.3 52.9 all-gather.2
